TPU v7x, 256 devices: a whole 4x4x8 slice. The times are simulated.
256 devices in a mesh: row: 16 (over x, y_lo, core), col: 16 (over y_hi, z).
Axes of the slice: x: 4, y: 4 (y_hi: 2, y_lo: 2; y = y_hi * 2 + y_lo), z: 8, core: 2. Of those that a mesh axis runs over, the one named last changes fastest.
Arguments:
- coeffs: bfloat16 [4096, 4096], P('row', 'col'), may hold values from -6 to 6
- block_tiles: bfloat16 [64, 48, 64, 64], P('col', 'row'), may hold values from -0.15625 to 0.15625
- neighbours: int32 [64, 48], P('col'), may hold values from 0 to 63, as said below
- density: int32 [32], replicated, may hold values from 6 to 48, as said below
Outputs:
- filtered: bfloat16 [4096, 4096], P('row', 'col')
Inputs may be any that keep to these rules, and one draw needn't show every extreme that they name: `neighbours`: slot 0 of block row b holds b itself. Where 48 <= 64 the slots of one block row name distinct block rows; otherwise every block row is named in each row and some more than once, whose tiles then add. `density`: the number of leading live slots of every block row of a region; some region has 48 and some has 6 in every draw.
All inputs are finite; a program needn't handle non-finite values.
Results may differ from a plain program's by a relative error of at most 0.0054.
Values may be sent and summed in bfloat16 or wider, within the bound.
No kernel may reach another device: no remote copies, remote signals or barrier semaphores. Data moves between devices by JAX's collectives and lax.ppermute only.
A program may use at most 64 MiB of HBM per device.

v0:
```python
import jax
import jax.numpy as jnp
from jax import lax
from jax.sharding import PartitionSpec as P

STEPS = 3
REG_BLK = 2


def body(coeffs, block_tiles, neighbours, density):
    local_width = coeffs.shape[0]
    block_rows = neighbours.shape[0]
    slot_count = neighbours.shape[1]
    block_size = block_tiles.shape[2]
    block_ids = lax.axis_index("col") * block_rows + jnp.arange(block_rows, dtype=jnp.int32)
    region_ids = block_ids // REG_BLK
    region_match = region_ids[:, None] == jnp.arange(density.shape[0], dtype=jnp.int32)[None, :]
    live_counts = jnp.sum(jnp.where(region_match, density[None, :], 0), axis=1)
    live_mask = jnp.arange(slot_count, dtype=jnp.int32)[None, :] < live_counts[:, None]

    def accumulate(blocks, tile_piece):
        piece_slots = tile_piece.shape[1]
        gathered = jnp.take(blocks, neighbours.reshape(-1), axis=1)
        gathered = gathered.reshape(local_width, block_rows, piece_slots, block_size)
        masked = jnp.where(live_mask[:, :, None, None], tile_piece, jnp.zeros((), tile_piece.dtype))
        return jnp.einsum("mbsj,bsij->mbi", gathered, masked, preferred_element_type=jnp.float32)

    def guarded(blocks, tile_piece):
        return accumulate(blocks, tile_piece)

    def apply_hamiltonian(current_field):
        all_coeffs = lax.all_gather(current_field, "col", axis=1, tiled=True)
        blocks = all_coeffs.reshape(local_width, -1, block_size)
        running = guarded(blocks, lax.all_gather(block_tiles, "row", axis=1, tiled=True))
        return running.reshape(local_width, block_rows * block_size)

    previous = coeffs
    current = apply_hamiltonian(coeffs).astype(jnp.bfloat16)
    for repeat in range(STEPS - 1):
        product = apply_hamiltonian(current)
        following = (2.0 * product - previous.astype(jnp.float32)).astype(jnp.bfloat16)
        previous = current
        current = following
    return current


def solution(mesh):
    placed = (P("row", "col"), P("col", "row", None, None), P("col", None), P())
    return jax.shard_map(
        body, mesh=mesh, in_specs=placed, out_specs=P("row", "col"), check_vma=False
    )
```

profile of v0, /device:TPU:2, one launch (start us, length us, event | category | flops | bytes accessed | tf_op | source)
XLA Modules:
  0.0 346.5 jit_solution(15413313421211487123)
XLA Ops:
  6.5 0.0 all-gather.7.cloned.1.call-start
  6.5 1.7 copy.14
  8.2 0.0 all-gather.7.cloned.1.call-update
  8.2 0.0 all-gather.5.cloned.1.call-start
  8.3 0.7 all-gather.5.cloned.1.call-update
  9.0 0.0 all-gather.9.cloned.1.call-start
  9.0 0.8 reshape.78
  9.8 0.8 select_reduce_fusion
  10.7 0.1 iota_compare_fusion.1
  10.8 87.5 %all-gather.7.cloned.1.call-done = bf16[256,4096]{0,1:T(8,128)(2,1)} async-done(((bf16[256,256]{0,1:T(8,128)(2,1)}), bf16[256,4096]{0,1:T(8,128)(2,1)}) %all-gather.7.cloned.1.call-update) | async-done | bytes 2097168 | tf_op jit(solution)/shard_map/all_gather | solution.py:32
  98.2 9.6 %gather_fusion = bf16[192,256,64]{1,2,0:T(8,128)(2,1)} fusion(bf16[256,64,64]{0,2,1:T(8,128)(2,1)} %bitcast.42, s32[1024]{0:T(1024)S(1)} %pad_clamp_fusion), kind=kCustom, calls=%fused_computation.clone | custom fusion | bytes 12583680 | tf_op jit(solution)/shard_map/jit(_take)/gather | solution.py:23
  107.8 6.2 %broadcast_select_fusion = bf16[192,256,64]{1,2,0:T(8,128)(2,1)} fusion(bf16[192,256,64]{1,2,0:T(8,128)(2,1)} %gather_fusion, pred[192]{0:T(512)(128)(4,1)S(1)} %compare_and_fusion), kind=kLoop, calls=%fused_computation.3 | loop fusion | flops 3145728 | bytes 12583104 | tf_op jit(solution)/shard_map/jit(_take)/select_n | solution.py:23
  114.1 20.3 %all-gather.5.cloned.1.call-done = bf16[4,48,64,64]{3,2,1,0:T(8,128)(2,1)} async-done(((bf16[4,3,64,64]{3,2,1,0:T(8,128)(2,1)}), bf16[4,48,64,64]{3,2,1,0:T(8,128)(2,1)}) %all-gather.5.cloned.1.call-update) | async-done | bytes 1572880 | tf_op jit(solution)/shard_map/all_gather | solution.py:34
  134.3 5.9 %fusion.11 = bf16[4,64,256]{2,1,0:T(8,128)(2,1)} fusion(bf16[256,4,48,64]{0,3,2,1:T(8,128)(2,1)} %bitcast.45, bf16[4,48,64,64]{3,2,1,0:T(8,128)(2,1)} %all-gather.5.cloned.1.call-done, pred[4,48]{1,0:T(4,128)(4,1)S(1)} %iota_compare_fusion.1), kind=kOutput, calls=%fused_computation.18 | convolution fusion | flops 403505152 | bytes 7995584 | tf_op jit(solution)/shard_map/mbsj,bsij->mbi/dot_general | solution.py:26
  140.2 0.0 all-gather.9.cloned.1.call-update
  140.3 0.2 all-gather.11.cloned.1.call-start
  140.5 85.6 %all-gather.9.cloned.1.call-done = bf16[256,4096]{0,1:T(8,128)(2,1)} async-done(((bf16[256,256]{0,1:T(8,128)(2,1)}), bf16[256,4096]{0,1:T(8,128)(2,1)}) %all-gather.9.cloned.1.call-update) | async-done | bytes 2097168 | tf_op jit(solution)/shard_map/all_gather | solution.py:32
  226.1 9.6 %gather_fusion.1 = bf16[192,256,64]{1,2,0:T(8,128)(2,1)} fusion(bf16[256,64,64]{0,2,1:T(8,128)(2,1)} %bitcast.44, s32[1024]{0:T(1024)S(1)} %pad_clamp_fusion), kind=kCustom, calls=%fused_computation.1.clone | custom fusion | bytes 12583680 | tf_op jit(solution)/shard_map/jit(_take)/gather | solution.py:23
  235.8 3.6 %broadcast_select_fusion.1 = bf16[192,256,64]{1,2,0:T(8,128)(2,1)S(1)} fusion(bf16[192,256,64]{1,2,0:T(8,128)(2,1)} %gather_fusion.1, pred[192]{0:T(512)(128)(4,1)S(1)} %compare_and_fusion), kind=kLoop, calls=%fused_computation.4 | loop fusion | flops 3145728 | bytes 12583104 | tf_op jit(solution)/shard_map/jit(_take)/select_n | solution.py:23
  239.4 0.0 copy-start
  239.4 0.1 copy-done.2
  239.5 1.7 fusion.10
  241.2 0.7 fusion.12
  241.9 0.0 all-gather.11.cloned.1.call-update
  241.9 0.1 copy.16
  242.0 82.1 %all-gather.11.cloned.1.call-done = bf16[256,4096]{0,1:T(8,128)(2,1)} async-done(((bf16[256,256]{0,1:T(8,128)(2,1)}), bf16[256,4096]{0,1:T(8,128)(2,1)}) %all-gather.11.cloned.1.call-update) | async-done | bytes 2097168 | tf_op jit(solution)/shard_map/all_gather | solution.py:32
  324.1 9.6 %gather_fusion.2 = bf16[192,256,64]{1,2,0:T(8,128)(2,1)} fusion(bf16[256,64,64]{0,2,1:T(8,128)(2,1)} %bitcast.43, s32[1024]{0:T(1024)S(1)} %pad_clamp_fusion), kind=kCustom, calls=%fused_computation.2.clone | custom fusion | bytes 12583680 | tf_op jit(solution)/shard_map/jit(_take)/gather | solution.py:23
  333.7 3.6 %broadcast_select_fusion.2 = bf16[192,256,64]{1,2,0:T(8,128)(2,1)S(1)} fusion(bf16[192,256,64]{1,2,0:T(8,128)(2,1)} %gather_fusion.2, pred[192]{0:T(512)(128)(4,1)S(1)} %compare_and_fusion), kind=kLoop, calls=%fused_computation.5 | loop fusion | flops 3145728 | bytes 12583104 | tf_op jit(solution)/shard_map/jit(_take)/select_n | solution.py:23
  337.3 0.1 copy-done.3
  337.4 1.7 fusion.9
  339.1 0.1 copy.17
  339.3 0.7 subtract_convert_fusion
  (9 shorter events, 0.0 us)
Async XLA Ops:
  6.5 91.7 %all-gather.7.cloned.1.call-start = ((), (), s32[]{:S(2)}) async-start(), calls=%async_computation.1 | async-start | bytes 2228224 | tf_op jit(solution)/shard_map/all_gather | solution.py:32
  8.2 126.1 %all-gather.5.cloned.1.call-start = ((), (), s32[]{:S(2)}) async-start(), calls=%async_computation | async-start | bytes 3342336 | tf_op jit(solution)/shard_map/all_gather | solution.py:34
  9.0 217.2 %all-gather.9.cloned.1.call-start = ((), (), s32[]{:S(2)}) async-start(), calls=%async_computation.2 | async-start | bytes 2228224 | tf_op jit(solution)/shard_map/all_gather | solution.py:32
  140.3 183.8 %all-gather.11.cloned.1.call-start = ((), (), s32[]{:S(2)}) async-start(), calls=%async_computation.3 | async-start | bytes 2228224 | tf_op jit(solution)/shard_map/all_gather | solution.py:32
  235.8 3.7 %copy-start.2 = (bf16[4,48,64,64]{3,2,1,0:T(8,128)(2,1)S(1)}, bf16[4,48,64,64]{3,2,1,0:T(8,128)(2,1)}, u32[]{:S(2)}) copy-start(bf16[4,48,64,64]{3,2,1,0:T(8,128)(2,1)} %all-gather.5.cloned.1.call-done) | copy-start | bytes 4718596
  239.4 1.8 copy-start
  239.4 2.5 copy-start.1
  333.7 3.7 %copy-start.3 = (bf16[4,48,64,64]{3,2,1,0:T(8,128)(2,1)S(1)}, bf16[4,48,64,64]{3,2,1,0:T(8,128)(2,1)}, u32[]{:S(2)}) copy-start(bf16[4,48,64,64]{3,2,1,0:T(8,128)(2,1)} %all-gather.5.cloned.1.call-done) | copy-start | bytes 4718596
Sparse Core Ops, SparseCore 0:
  9.9 88.2 all-gather.6
  100.0 34.2 all-gather.4
  140.4 85.6 all-gather.8
  242.0 82.0 all-gather.10
where the time goes:
time: 347 us; the launch traced here: 346 us
  waiting for transfers between devices  276 us (80%)
  local copies, waits for them, and re-layouts  31.8 us (9%)
  other arithmetic  15.7 us (5%)
  between operations  13.2 us (4%)
  matrix products  9.31 us (3%)
    all_gather x3, waiting for transfers between devices, apply_hamiltonian(): all_coeffs = lax.all_gather(current_field, 'col', axis=1, tiled=True)  255 us
    gather x3, local copies, waits for them, and re-layouts, accumulate(): gathered = jnp.take(blocks, neighbours.reshape(-1), axis=1)  28.9 us
    all_gather x1, waiting for transfers between devices, apply_hamiltonian(): lax.all_gather(block_tiles, 'row', axis=1, tiled=True)  20.3 us
    select_n x4, other arithmetic, accumulate(): gathered = jnp.take(blocks, neighbours.reshape(-1), axis=1)  13.4 us
    dot_general x3, matrix products, accumulate(): jnp.einsum('mbsj,bsij->mbi', gathered, masked, preferred_element_type=jnp...  9.31 us
  transfers between devices with their start and end apart: 4, of which 4 were waited for; matrix products, arithmetic and copies ran while one was open for 5% of the time, Pallas kernels for 0%

commit v1 on v0

--- a/solution.py
+++ b/solution.py
@@ -31,7 +31,12 @@
     def apply_hamiltonian(current_field):
         all_coeffs = lax.all_gather(current_field, "col", axis=1, tiled=True)
         blocks = all_coeffs.reshape(local_width, -1, block_size)
-        running = guarded(blocks, lax.all_gather(block_tiles, "row", axis=1, tiled=True))
+        running = guarded(
+            blocks,
+            jnp.concatenate(
+                lax.all_to_all(jnp.stack([block_tiles] * lax.axis_size("row")), "row", 0, 0), axis=1
+            ),
+        )
         return running.reshape(local_width, block_rows * block_size)
 
     previous = coeffs

time: 347 us -> 327 us (0.942)
  waiting for transfers between devices: 276 us -> 245 us
  local copies, waits for them, and re-layouts: 31.8 us -> 43.4 us
  starting transfers between devices: 0.3 us -> 6.65 us
  other arithmetic: 15.7 us -> 12.1 us
    all_gather x3, waiting for transfers between devices: 255 us -> 225 us  [apply_hamiltonian(): all_coeffs = lax.all_gather(current_field, 'col', axis=1, tiled=True)]
    all_gather x1 -> x0, waiting for transfers between devices: 20.3 us -> none  [apply_hamiltonian(): lax.all_gather(block_tiles, 'row', axis=1, tiled=True)]
    all_to_all x0 -> x1, waiting for transfers between devices: none -> 19.9 us  [apply_hamiltonian(): lax.all_to_all(jnp.stack([block_tiles] * lax.axis_size('row')), 'row', 0, 0)]
    unnamed x9 -> x13, local copies, waits for them, and re-layouts: 1.89 us -> 8.83 us
    all_to_all x0 -> x1, starting transfers between devices: none -> 6.39 us  [apply_hamiltonian(): lax.all_to_all(jnp.stack([block_tiles] * lax.axis_size('row')), 'row', 0, 0)]
  transfers between devices with their start and end apart: 4 -> 4, of which waited for: 4 -> 4; matrix products, arithmetic and copies ran while one was open for 5% -> 4% of each run, Pallas kernels for 0% -> 0%
where the time goes in v1:
time: 327 us
  waiting for transfers between devices  245 us (75%)
  local copies, waits for them, and re-layouts  43.4 us (13%)
  between operations  13.2 us (4%)
  other arithmetic  12.1 us (4%)
  starting transfers between devices  6.65 us (2%)
  matrix products  6.22 us (2%)
    all_gather x3, waiting for transfers between devices, apply_hamiltonian(): all_coeffs = lax.all_gather(current_field, 'col', axis=1, tiled=True)  225 us
    gather x3, local copies, waits for them, and re-layouts, accumulate(): gathered = jnp.take(blocks, neighbours.reshape(-1), axis=1)  28.9 us
    all_to_all x1, waiting for transfers between devices, apply_hamiltonian(): lax.all_to_all(jnp.stack([block_tiles] * lax.axis_size('row')), 'row', 0, 0)  19.9 us
    select_n x4, other arithmetic, accumulate(): gathered = jnp.take(blocks, neighbours.reshape(-1), axis=1)  10.4 us
    unnamed x13, local copies, waits for them, and re-layouts  8.83 us
  transfers between devices with their start and end apart: 4, of which 4 were waited for; matrix products, arithmetic and copies ran while one was open for 4% of the time, Pallas kernels for 0%

profile of v1, /device:TPU:2, one launch (start us, length us, event | category | flops | bytes accessed | tf_op | source)
XLA Modules:
  0.0 326.6 jit_solution(1868336615458525614)
XLA Ops:
  6.5 1.7 copy.24
  8.2 0.0 all-gather.4.cloned.1.call-update
  8.3 1.7 stack.2
  10.0 3.2 reshape.134
  13.2 6.4 %all-to-all-start = ((bf16[16,2,24576]{2,1,0:T(2,128)(2,1)}), bf16[16,2,24576]{2,1,0:T(2,128)(2,1)}, u32[]{:S(2)}, u32[]{:S(2)}) async-start(bf16[16,2,24576]{2,1,0:T(2,128)(2,1)} %reshape.134), calls=%async_computation | async-start | bytes 3145728 | tf_op jit(solution)/shard_map/all_to_all | solution.py:37
  19.6 0.0 all-gather.6.cloned.1.call-start
  19.7 0.1 reshape.92
  19.8 0.2 select_reduce_fusion
  20.0 0.1 iota_compare_fusion.1
  20.0 19.9 %all-to-all-done = bf16[16,2,24576]{2,1,0:T(2,128)(2,1)} async-done(((bf16[16,2,24576]{2,1,0:T(2,128)(2,1)}), bf16[16,2,24576]{2,1,0:T(2,128)(2,1)}, u32[]{:S(2)}, u32[]{:S(2)}) %all-to-all-start) | async-done | bytes 1572896 | tf_op jit(solution)/shard_map/all_to_all | solution.py:37
  40.0 3.8 %reshape.135 = bf16[16,4,3,64,64]{4,3,2,1,0:T(8,128)(2,1)S(1)} reshape(bf16[16,2,24576]{2,1,0:T(2,128)(2,1)} %all-to-all-done) | data formatting | bytes 3145728
  43.8 2.7 copy.23
  46.4 61.1 %all-gather.4.cloned.1.call-done = bf16[256,4096]{0,1:T(8,128)(2,1)} async-done(((bf16[256,256]{0,1:T(8,128)(2,1)}), bf16[256,4096]{0,1:T(8,128)(2,1)}) %all-gather.4.cloned.1.call-update) | async-done | bytes 2097168 | tf_op jit(solution)/shard_map/all_gather | solution.py:32
  107.5 9.6 %gather_fusion = bf16[192,256,64]{1,2,0:T(8,128)(2,1)} fusion(bf16[256,64,64]{0,2,1:T(8,128)(2,1)} %bitcast.45, s32[1024]{0:T(1024)S(1)} %pad_clamp_fusion), kind=kCustom, calls=%fused_computation.clone | custom fusion | bytes 12583680 | tf_op jit(solution)/shard_map/jit(_take)/gather | solution.py:23
  117.1 3.6 %broadcast_select_fusion = bf16[192,256,64]{1,2,0:T(8,128)(2,1)S(1)} fusion(bf16[192,256,64]{1,2,0:T(8,128)(2,1)} %gather_fusion, pred[192]{0:T(512)(128)(4,1)S(1)} %compare_and_fusion), kind=kLoop, calls=%fused_computation.3 | loop fusion | flops 3145728 | bytes 12583104 | tf_op jit(solution)/shard_map/jit(_take)/select_n | solution.py:23
  120.7 0.1 copy-done
  120.9 2.2 fusion.11
  123.1 0.0 all-gather.6.cloned.1.call-update
  123.1 0.2 all-gather.8.cloned.1.call-start
  123.3 82.0 %all-gather.6.cloned.1.call-done = bf16[256,4096]{0,1:T(8,128)(2,1)} async-done(((bf16[256,256]{0,1:T(8,128)(2,1)}), bf16[256,4096]{0,1:T(8,128)(2,1)}) %all-gather.6.cloned.1.call-update) | async-done | bytes 2097168 | tf_op jit(solution)/shard_map/all_gather | solution.py:32
  205.3 9.6 %gather_fusion.1 = bf16[192,256,64]{1,2,0:T(8,128)(2,1)} fusion(bf16[256,64,64]{0,2,1:T(8,128)(2,1)} %bitcast.47, s32[1024]{0:T(1024)S(1)} %pad_clamp_fusion), kind=kCustom, calls=%fused_computation.1.clone | custom fusion | bytes 12583680 | tf_op jit(solution)/shard_map/jit(_take)/gather | solution.py:23
  214.9 3.4 %broadcast_select_fusion.1 = bf16[192,256,64]{1,2,0:T(8,128)(2,1)S(1)} fusion(bf16[192,256,64]{1,2,0:T(8,128)(2,1)} %gather_fusion.1, pred[192]{0:T(512)(128)(4,1)S(1)} %compare_and_fusion), kind=kLoop, calls=%fused_computation.4 | loop fusion | flops 3145728 | bytes 12583104 | tf_op jit(solution)/shard_map/jit(_take)/select_n | solution.py:23
  218.4 1.7 fusion.10
  220.1 0.7 fusion.12
  220.8 0.0 all-gather.8.cloned.1.call-update
  220.8 0.1 copy.26
  220.9 82.1 %all-gather.8.cloned.1.call-done = bf16[256,4096]{0,1:T(8,128)(2,1)} async-done(((bf16[256,256]{0,1:T(8,128)(2,1)}), bf16[256,4096]{0,1:T(8,128)(2,1)}) %all-gather.8.cloned.1.call-update) | async-done | bytes 2097168 | tf_op jit(solution)/shard_map/all_gather | solution.py:32
  303.0 9.6 %gather_fusion.2 = bf16[192,256,64]{1,2,0:T(8,128)(2,1)} fusion(bf16[256,64,64]{0,2,1:T(8,128)(2,1)} %bitcast.46, s32[1024]{0:T(1024)S(1)} %pad_clamp_fusion), kind=kCustom, calls=%fused_computation.2.clone | custom fusion | bytes 12583680 | tf_op jit(solution)/shard_map/jit(_take)/gather | solution.py:23
  312.6 3.4 %broadcast_select_fusion.2 = bf16[192,256,64]{1,2,0:T(8,128)(2,1)S(1)} fusion(bf16[192,256,64]{1,2,0:T(8,128)(2,1)} %gather_fusion.2, pred[192]{0:T(512)(128)(4,1)S(1)} %compare_and_fusion), kind=kLoop, calls=%fused_computation.5 | loop fusion | flops 3145728 | bytes 12583104 | tf_op jit(solution)/shard_map/jit(_take)/select_n | solution.py:23
  316.1 2.3 fusion.9
  318.3 1.1 copy.27
  319.4 0.7 subtract_convert_fusion
  (14 shorter events, 0.0 us)
Async XLA Ops:
  6.5 13.1 %copy-start.3 = (s32[4,48]{1,0:T(4,128)S(1)}, s32[4,48]{1,0:T(4,128)}, u32[]{:S(2)}) copy-start(s32[4,48]{1,0:T(4,128)} %param.8) | copy-start | bytes 2308
  6.5 13.2 %copy-start.4 = (s32[32]{0:T(128)S(1)}, s32[32]{0:T(128)}, u32[]{:S(2)}) copy-start(s32[32]{0:T(128)} %param.9) | copy-start | bytes 388
  6.5 101.0 %all-gather.4.cloned.1.call-start = ((), (), s32[]{:S(2)}) async-start(), calls=%async_computation.1 | async-start | bytes 2228224 | tf_op jit(solution)/shard_map/all_gather | solution.py:32
  13.2 26.8 %all-to-all-start = ((bf16[16,2,24576]{2,1,0:T(2,128)(2,1)}), bf16[16,2,24576]{2,1,0:T(2,128)(2,1)}, u32[]{:S(2)}, u32[]{:S(2)}) async-start(bf16[16,2,24576]{2,1,0:T(2,128)(2,1)} %reshape.134), calls=%async_computation | async-start | bytes 3145728 | tf_op jit(solution)/shard_map/all_to_all | solution.py:37
  19.6 185.7 %all-gather.6.cloned.1.call-start = ((), (), s32[]{:S(2)}) async-start(), calls=%async_computation.2 | async-start | bytes 2228224 | tf_op jit(solution)/shard_map/all_gather | solution.py:32
  117.1 3.7 %copy-start = (bf16[16,4,3,64,64]{4,3,2,0,1:T(8,128)(2,1)S(1)}, bf16[16,4,3,64,64]{4,3,2,0,1:T(8,128)(2,1)}, u32[]{:S(2)}) copy-start(bf16[16,4,3,64,64]{4,3,2,0,1:T(8,128)(2,1)} %copy.23) | copy-start | bytes 4718596
  123.1 179.9 %all-gather.8.cloned.1.call-start = ((), (), s32[]{:S(2)}) async-start(), calls=%async_computation.3 | async-start | bytes 2228224 | tf_op jit(solution)/shard_map/all_gather | solution.py:32
  218.3 1.8 copy-start.1
  218.4 2.5 copy-start.2
Sparse Core Ops, SparseCore 0:
  9.9 97.5 all-gather.3
  123.2 82.0 all-gather.5
  220.9 82.0 all-gather.7
